TPU v7x, 32 devices: a whole 2x2x4 slice. The times are simulated.
32 devices in a mesh: shot: 8 (over z, y), off: 4 (over x, core).
Axes of the slice: x: 2, y: 2, z: 4, core: 2. Of those that a mesh axis runs over, the one named last changes fastest.
Arguments:
- traces: float32 [8192, 2048], P(('shot', 'off')), may hold values from -6 to 6
- cmp_bin: int32 [8192], P(('shot', 'off')), may hold values from 0 to 255, as said below
- offset_class: int32 [8192], P(('shot', 'off')), may hold values from 0 to 79, as said below
- bin_rank: int32 [256], replicated, may hold values from 0 to 255, as said below
- filter_off: float32 [7], replicated, may hold values from -2.5 to 2.5
- filter_time: float32 [65], replicated, may hold values from -2 to 2
Outputs:
- planes: float32 [80, 2048, 256], P('off', 'shot')
Inputs may be any that keep to these rules, and one draw needn't show every extreme that they name: `cmp_bin`: in each aligned block of 256 rows (the rows of one device) at most 128 rows name bins with the same owner bin_rank // 32; one owner, the same for all blocks, gets exactly 128 rows of every block, and every other owner gets a whole number of rows next to 128 / (7) (its floor or ceiling). `offset_class`: row r has a class from g * 20 to g * 20 + 19, with g = (r // 256) % 4. `bin_rank`: A permutation.
All inputs are finite; a program needn't handle non-finite values.
Results may differ from a plain program's by a relative error of at most 0.00007.
Values sent between devices are 32-bit elements; how exact they have to be, the bound alone decides.
No kernel may reach another device: no remote copies, remote signals or barrier semaphores. Data moves between devices by JAX's collectives and lax.ppermute only.
A program may use at most 128 MiB of HBM per device.

v0:
```python
import jax
import jax.numpy as jnp
from jax import lax
from jax.sharding import PartitionSpec as P

OFFC = 80
BOWN = 32


def extended_2(cells, sides, width):
    for axis, dim in sides:
        count = lax.axis_size(axis)
        ends = count - 1
        head = lax.slice_in_dim(cells, 0, width, axis=dim)
        tail = lax.slice_in_dim(cells, cells.shape[dim] - width, cells.shape[dim], axis=dim)
        cells = jnp.concatenate(
            [
                lax.ppermute(tail, axis, [(i, (i + 1) % count) for i in range(ends)]),
                cells,
                lax.ppermute(head, axis, [((i + 1) % count, i) for i in range(ends)]),
            ],
            axis=dim,
        )
    return cells


def tap_table(filter_time, width_in, width_out):
    inner = jnp.arange(width_in, dtype=jnp.int32)[:, None]
    outer = jnp.arange(width_out, dtype=jnp.int32)[None, :]
    distance = inner - outer
    taps = jnp.arange(filter_time.shape[0], dtype=jnp.int32)
    matches = distance[:, :, None] == taps[None, None, :]
    return jnp.sum(jnp.where(matches, filter_time[None, None, :], 0.0), axis=2)


def block_filter(data, filter_time):
    reach = filter_time.shape[0] // 2
    block_width = 128
    leading = data.shape[:-1]
    samples = data.shape[-1]
    blocks = data.reshape(leading + (samples // block_width, block_width))
    zeroes = jnp.zeros(leading + (1, reach), jnp.float32)
    before = jnp.concatenate([zeroes, blocks[..., :-1, block_width - reach :]], axis=-2)
    after = jnp.concatenate([blocks[..., 1:, :reach], zeroes], axis=-2)
    extended = jnp.concatenate([before, blocks, after], axis=-1)
    table = tap_table(filter_time, block_width + 2 * reach, block_width)
    result = jnp.einsum("...ki,io->...ko", extended, table, precision=lax.Precision.HIGHEST)
    return result.reshape(leading + (samples,))


def offset_mix(scaled, filter_off):
    reach = filter_off.shape[0] // 2
    padded = extended_2(scaled, (("off", 0),), reach)
    count = scaled.shape[0]
    mixed = filter_off[0] * padded[0:count]
    for offset_tap in range(1, filter_off.shape[0]):
        mixed = mixed + filter_off[offset_tap] * padded[offset_tap : offset_tap + count]
    return mixed


def stack_cells(received, labels, segments):
    stacked = jax.ops.segment_sum(received, labels, num_segments=segments + 1)[:segments]
    fold_count = jax.ops.segment_sum(
        jnp.ones(labels.shape, jnp.float32), labels, num_segments=segments + 1
    )[:segments]
    return stacked / jnp.maximum(fold_count, 1.0)[:, None]


def body(traces, cmp_bin, offset_class, bin_rank, filter_off, filter_time):
    shots = lax.axis_size("shot")
    off_dev = OFFC // lax.axis_size("off")
    first_class = lax.axis_index("off") * off_dev
    bin_count = bin_rank.shape[0]
    tr_dev = traces.shape[0]
    samples = traces.shape[1]
    matches = cmp_bin[:, None] == jnp.arange(bin_count, dtype=jnp.int32)[None, :]
    rank_of = jnp.sum(jnp.where(matches, bin_rank[None, :], 0), axis=1)
    local_class = offset_class - first_class
    capacity = max(2, 4 * tr_dev // shots)
    owning = rank_of // BOWN
    member = (owning[:, None] == jnp.arange(shots, dtype=jnp.int32)[None, :]).astype(jnp.int32)
    position = jnp.sum(jnp.cumsum(member, axis=0) * member, axis=1) - 1
    target = owning * capacity + position
    sentinel = off_dev * BOWN
    cell_index = local_class * BOWN + rank_of % BOWN
    outgoing = jnp.zeros((shots * capacity, samples), jnp.float32).at[target].set(traces)
    labels = jnp.full((shots * capacity,), sentinel, jnp.int32).at[target].set(cell_index)
    received, arrived = (
        lax.all_to_all(outgoing, "shot", split_axis=0, concat_axis=0, tiled=True),
        lax.all_to_all(labels, "shot", split_axis=0, concat_axis=0, tiled=True),
    )
    scaled = stack_cells(received, arrived, sentinel).reshape(off_dev, BOWN, samples)
    mixed = offset_mix(scaled, filter_off)
    filtered = block_filter(mixed, filter_time)
    relayed = lax.all_to_all(filtered, "shot", split_axis=2, concat_axis=1, tiled=True)
    return jnp.transpose(relayed, (0, 2, 1))


def solution(mesh):
    return jax.shard_map(
        body,
        mesh=mesh,
        in_specs=(P(("shot", "off"), None), P(("shot", "off")), P(("shot", "off")), P(), P(), P()),
        out_specs=P("off", "shot", None),
        check_vma=False,
    )
```

profile of v0, /device:TPU:1, one launch (start us, length us, event | category | flops | bytes accessed | tf_op | source)
XLA Modules:
  0.0 474.5 jit_solution(17869726358721929491)
XLA Ops:
  0.0 0.9 select_reduce_fusion.1
  2.6 2.0 scatter_custom_fusion
  4.5 6.4 %all-to-all-start = ((s32[8,128,1]{1,2,0:T(1,128)}), s32[8,128,1]{1,2,0:T(1,128)S(1)}, u32[]{:S(2)}, u32[]{:S(2)}) async-start(s32[8,128,1]{1,2,0:T(1,128)} %bitcast.8), calls=%async_computation | async-start | bytes 8192 | tf_op jit(solution)/shard_map/all_to_all | solution.py:90
  10.9 6.6 %scatter_custom_fusion.1 = f32[1024,2048]{1,0:T(8,128)} fusion(s32[256]{0:T(256)S(1)} %bitcast.67, f32[256,2048]{1,0:T(8,128)} %param.6, f32[]{:T(128)} %constant.24.clone.1), kind=kCustom, calls=%fused_computation.44 | custom fusion | bytes 8389120 | tf_op jit(solution)/shard_map/scatter | solution.py:86
  17.5 5.4 %all-to-all-start.1 = ((f32[8,128,2048]{2,1,0:T(8,128)}), f32[8,128,2048]{2,1,0:T(8,128)}, u32[]{:S(2)}, u32[]{:S(2)}) async-start(f32[8,128,2048]{2,1,0:T(8,128)} %bitcast.56), calls=%async_computation.1 | async-start | bytes 16777216 | tf_op jit(solution)/shard_map/all_to_all | solution.py:89
  22.9 8.1 %scatter_custom_fusion.3 = f32[641]{0:T(1024)S(1)} fusion(s32[1024]{0:T(1024)S(1)} %bitcast.64, f32[1024]{0:T(1024)S(1)} %broadcast.160, f32[]{:T(128)} %constant.24.clone.1), kind=kCustom, calls=%fused_computation.64 | custom fusion | flops 1024 | bytes 2568 | tf_op jit(solution)/shard_map/scatter-add | solution.py:63
  31.0 173.6 %all-to-all-done.1 = f32[8,128,2048]{2,1,0:T(8,128)} async-done(((f32[8,128,2048]{2,1,0:T(8,128)}), f32[8,128,2048]{2,1,0:T(8,128)}, u32[]{:S(2)}, u32[]{:S(2)}) %all-to-all-start.1) | async-done | bytes 8388640 | tf_op jit(solution)/shard_map/all_to_all | solution.py:89
  204.7 17.4 %scatter_custom_fusion.2 = f32[641,2048]{1,0:T(8,128)} fusion(s32[1024]{0:T(1024)S(1)} %bitcast.65, f32[1024,2048]{1,0:T(8,128)} %bitcast.11, f32[]{:T(128)} %constant.24.clone.1), kind=kCustom, calls=%fused_computation.46 | custom fusion | flops 2097152 | bytes 5251584 | tf_op jit(solution)/shard_map/scatter-add | solution.py:62
  222.1 3.3 slice_divide_fusion
  225.5 5.4 %collective-permute-start = (f32[3,32,2048]{2,1,0:T(8,128)S(1)}, f32[3,32,2048]{2,1,0:T(8,128)S(1)}, u32[]{:S(2)}, u32[]{:S(2)}) collective-permute-start(f32[3,32,2048]{2,1,0:T(8,128)S(1)} %bitcast.61), channel_id=1, source_target_pairs={{0,1},{1,2},{2,3},{4,5},{5,6},{6,7},{8,9},{9,10},{10,11},{12,13},{... | collective-permute-start | bytes 2359304 | tf_op jit(solution)/shard_map/ppermute | solution.py:18
  230.9 2.1 collective-permute-start.1
  234.5 5.3 %collective-permute-done = f32[3,32,2048]{2,1,0:T(8,128)S(1)} collective-permute-done((f32[3,32,2048]{2,1,0:T(8,128)S(1)}, f32[3,32,2048]{2,1,0:T(8,128)S(1)}, u32[]{:S(2)}, u32[]{:S(2)}) %collective-permute-start) | collective-permute-done | bytes 786464 | tf_op jit(solution)/shard_map/ppermute | solution.py:18
  239.8 4.4 collective-permute-done.1
  244.2 8.8 %fusion.7 = f32[20,32,2048]{2,1,0:T(8,128)S(1)} fusion(f32[20,32,2048]{2,1,0:T(8,128)S(1)} %bitcast.57, f32[3,32,2048]{2,1,0:T(8,128)S(1)} %collective-permute-done.1, f32[3,32,2048]{2,1,0:T(8,128)S(1)} %collective-permute-done, f32[]{:T(128)} %bitcast.20, f32[]{:T(128)} %bitcast.19, f32[]{:T(128)} %bitcast.17, f32[]{:T(128)} %bitcast.16, f32[]{:T(128)} %bitcast.15, ...), kind=kLoop, calls=%fused_computation.25 | loop fusion | flops 24903680 | bytes 12058652 | tf_op jit(solution)/shard_map/add | solution.py:57
  253.0 1.2 copy.25
  254.2 4.2 fusion.39
  258.4 13.8 %fusion = f32[20,32,16,128]{3,2,1,0:T(8,128)} fusion(f32[20,32,15,32]{3,2,1,0:T(8,128)} %get-tuple-element.6, f32[20,32,15,32]{3,2,1,0:T(8,128)S(1)} %get-tuple-element.5, f32[20,32,16,128]{3,2,1,0:T(8,128)S(1)} %bitcast.55, f32[192,128]{1,0:T(8,128)S(1)} %select_reduce_fusion), kind=kOutput, calls=%fused_computation.5 | convolution fusion | flops 3031695360 | bytes 13041664 | tf_op jit(solution)/shard_map/...ki,io->...ko/dot_general | solution.py:47
  272.3 13.1 %copy.22 = f32[20,32,16,128]{1,0,3,2:T(8,128)} copy(f32[20,32,16,128]{3,2,1,0:T(8,128)} %fusion) | data formatting | bytes 10485760 | tf_op jit(solution)/shard_map/reshape | solution.py:48
  285.4 16.2 %reshape.172 = f32[8,1,163840]{2,1,0:T(1,128)} reshape(f32[2048,20,32]{2,1,0:T(8,128)} %bitcast.52) | data formatting | bytes 10485760
  301.6 111.8 %all_to_all.39 = f32[8,1,163840]{2,1,0:T(1,128)} all-to-all(f32[8,1,163840]{2,1,0:T(1,128)} %reshape.172), channel_id=1, replica_groups=mesh['shot'=8,'off'=4] {'shot'}, dimensions={0} | all-to-all | bytes 10485760 | tf_op jit(solution)/shard_map/all_to_all | solution.py:95
  413.9 16.8 %reduce.2 = f32[8,163840]{1,0:T(8,128)} reduce(f32[8,1,163840]{2,1,0:T(1,128)} %all_to_all.39, f32[]{:T(128)} %broadcast.208), dimensions={1}, to_apply=%all_to_all.32.reduce_sub_computation | reduce | bytes 10485764 | tf_op jit(solution)/shard_map/all_to_all | solution.py:95
  430.7 21.3 %reshape.173 = f32[2048,20,32]{2,1,0:T(8,128)} reshape(f32[8,163840]{1,0:T(8,128)} %reduce.2) | data formatting | bytes 10485760
  452.0 16.4 %copy.19 = f32[20,8,32,256]{3,2,1,0:T(8,128)} copy(f32[20,8,32,256]{2,0,3,1:T(8,128)} %bitcast.53) | data formatting | bytes 10485760 | tf_op jit(solution)/shard_map/all_to_all | solution.py:95
  468.4 5.9 %copy.20 = f32[20,256,256]{2,1,0:T(8,128)} copy(f32[20,256,256]{1,2,0:T(8,128)} %bitcast.59) | data formatting | bytes 10485760 | tf_op jit(solution)/shard_map/transpose | solution.py:96
  (22 shorter events, 3.8 us)
Async XLA Ops:
  4.5 13.0 %all-to-all-start = ((s32[8,128,1]{1,2,0:T(1,128)}), s32[8,128,1]{1,2,0:T(1,128)S(1)}, u32[]{:S(2)}, u32[]{:S(2)}) async-start(s32[8,128,1]{1,2,0:T(1,128)} %bitcast.8), calls=%async_computation | async-start | bytes 8192 | tf_op jit(solution)/shard_map/all_to_all | solution.py:90
  17.5 187.2 %all-to-all-start.1 = ((f32[8,128,2048]{2,1,0:T(8,128)}), f32[8,128,2048]{2,1,0:T(8,128)}, u32[]{:S(2)}, u32[]{:S(2)}) async-start(f32[8,128,2048]{2,1,0:T(8,128)} %bitcast.56), calls=%async_computation.1 | async-start | bytes 16777216 | tf_op jit(solution)/shard_map/all_to_all | solution.py:89
  222.0 10.9 %copy-start = (f32[7]{0:T(128)S(1)}, f32[7]{0:T(128)}, u32[]{:S(2)}) copy-start(f32[7]{0:T(128)} %param.10) | copy-start | bytes 88
  222.1 11.6 %copy-start.1 = (f32[65]{0:T(128)S(1)}, f32[65]{0:T(128)}, u32[]{:S(2)}) copy-start(f32[65]{0:T(128)} %param.11) | copy-start | bytes 784
  225.5 14.3 %collective-permute-start = (f32[3,32,2048]{2,1,0:T(8,128)S(1)}, f32[3,32,2048]{2,1,0:T(8,128)S(1)}, u32[]{:S(2)}, u32[]{:S(2)}) collective-permute-start(f32[3,32,2048]{2,1,0:T(8,128)S(1)} %bitcast.61), channel_id=1, source_target_pairs={{0,1},{1,2},{2,3},{4,5},{5,6},{6,7},{8,9},{9,10},{10,11},{12,13},{... | collective-permute-start | bytes 2359304 | tf_op jit(solution)/shard_map/ppermute | solution.py:18
  230.9 13.3 %collective-permute-start.1 = (f32[3,32,2048]{2,1,0:T(8,128)S(1)}, f32[3,32,2048]{2,1,0:T(8,128)S(1)}, u32[]{:S(2)}, u32[]{:S(2)}) collective-permute-start(f32[3,32,2048]{2,1,0:T(8,128)S(1)} %bitcast.60), channel_id=1, source_target_pairs={{1,0},{2,1},{3,2},{5,4},{6,5},{7,6},{9,8},{10,9},{11,10},{13,12},{... | collective-permute-start | bytes 2359304 | tf_op jit(solution)/shard_map/ppermute | solution.py:20
where the time goes:
time: 480 us; the launch traced here: 475 us
  waiting for transfers between devices  183 us (38%)
  blocking collectives  112 us (23%)
  local copies, waits for them, and re-layouts  88.5 us (18%)
  other arithmetic  57.4 us (12%)
  starting transfers between devices  19.3 us (4%)
  matrix products  13.8 us (3%)
    all_to_all x1, waiting for transfers between devices, body(): lax.all_to_all(outgoing, 'shot', split_axis=0, concat_axis=0, tiled=True)  174 us
    all_to_all x1, blocking collectives, body(): lax.all_to_all(filtered, 'shot', split_axis=2, concat_axis=1, tiled=True)  112 us
    unnamed x7, local copies, waits for them, and re-layouts  38.7 us
    scatter-add x1, other arithmetic, stack_cells(): jax.ops.segment_sum(received, labels, num_segments=segments + 1)[:segments]  17.4 us
    all_to_all x2, local copies, waits for them, and re-layouts, body(): lax.all_to_all(filtered, 'shot', split_axis=2, concat_axis=1, tiled=True)  16.9 us
    all_to_all x1, other arithmetic, body(): lax.all_to_all(filtered, 'shot', split_axis=2, concat_axis=1, tiled=True)  16.8 us
    dot_general x1, matrix products, block_filter(): jnp.einsum('...ki,io->...ko', extended, table, precision=lax.Precision.HI...  13.8 us
    reshape x1, local copies, waits for them, and re-layouts, block_filter(): return result.reshape(leading + (samples,))  13.1 us
  transfers between devices with their start and end apart: 4, of which 3 were waited for; matrix products, arithmetic and copies ran while one was open for 3% of the time, Pallas kernels for 0%

commit v1 on v0

--- a/solution.py
+++ b/solution.py
@@ -1,3 +1,4 @@
+import functools
 import jax
 import jax.numpy as jnp
 from jax import lax
@@ -5,6 +6,22 @@
 
 OFFC = 80
 BOWN = 32
+
+
+def wrap_pools(array_in, axis_name):
+    base_arr = jnp.concatenate(
+        lax.all_to_all(
+            jnp.stack(jnp.split(array_in, lax.axis_size(axis_name), axis=2)),
+            axis_name=axis_name,
+            split_axis=0,
+            concat_axis=0,
+        ),
+        axis=1,
+    )
+    return base_arr
+
+
+list_results = functools.partial(wrap_pools, axis_name="shot")
 
 
 def extended_2(cells, sides, width):
@@ -92,7 +109,7 @@
     scaled = stack_cells(received, arrived, sentinel).reshape(off_dev, BOWN, samples)
     mixed = offset_mix(scaled, filter_off)
     filtered = block_filter(mixed, filter_time)
-    relayed = lax.all_to_all(filtered, "shot", split_axis=2, concat_axis=1, tiled=True)
+    relayed = list_results(filtered)
     return jnp.transpose(relayed, (0, 2, 1))
 
 

time: 480 us -> 407 us (0.85); the launches traced: 475 us -> 406 us
  local copies, waits for them, and re-layouts: 88.5 us -> 39.5 us
  other arithmetic: 57.4 us -> 40.3 us
    unnamed x7 -> x12, local copies, waits for them, and re-layouts: 38.7 us -> 9.14 us
    all_to_all x1 -> x0, other arithmetic: 16.8 us -> none  [body(): lax.all_to_all(filtered, 'shot', split_axis=2, concat_axis=1, tiled=True)]
    all_to_all x2 -> x1, local copies, waits for them, and re-layouts: 16.9 us -> 2.75 us  [wrap_pools(): lax.all_to_all(jnp.stack(jnp.split(array_in, lax.axis_size(axis_name), ax...]
    reshape x1, local copies, waits for them, and re-layouts: 13.1 us -> 6.72 us  [block_filter(): return result.reshape(leading + (samples,))]
  transfers between devices with their start and end apart: 4 -> 4, of which waited for: 3 -> 3; matrix products, arithmetic and copies ran while one was open for 3% -> 4% of each run, Pallas kernels for 0% -> 0%
where the time goes in v1:
time: 407 us; the launch traced here: 406 us
  waiting for transfers between devices  181 us (44%)
  blocking collectives  112 us (28%)
  other arithmetic  40.3 us (10%)
  local copies, waits for them, and re-layouts  39.5 us (10%)
  starting transfers between devices  19.4 us (5%)
  matrix products  13.8 us (3%)
    all_to_all x1, waiting for transfers between devices, body(): lax.all_to_all(outgoing, 'shot', split_axis=0, concat_axis=0, tiled=True)  174 us
    all_to_all x1, blocking collectives, wrap_pools(): lax.all_to_all(jnp.stack(jnp.split(array_in, lax.axis_size(axis_name), ax...  112 us
    scatter-add x1, other arithmetic, stack_cells(): jax.ops.segment_sum(received, labels, num_segments=segments + 1)[:segments]  17.4 us
    dot_general x1, matrix products, block_filter(): jnp.einsum('...ki,io->...ko', extended, table, precision=lax.Precision.HI...  13.8 us
    unnamed x12, local copies, waits for them, and re-layouts  9.14 us
    add x1, other arithmetic, offset_mix(): mixed + filter_off[offset_tap] * padded[offset_tap:offset_tap + count]  8.77 us
  transfers between devices with their start and end apart: 4, of which 3 were waited for; matrix products, arithmetic and copies ran while one was open for 4% of the time, Pallas kernels for 0%

profile of v1, /device:TPU:1, one launch (start us, length us, event | category | flops | bytes accessed | tf_op | source)
XLA Modules:
  0.0 406.4 jit_solution(4111863124386256020)
XLA Ops:
  2.6 2.0 scatter_custom_fusion
  4.5 6.4 %all-to-all-start = ((s32[8,128,1]{1,2,0:T(1,128)}), s32[8,128,1]{1,2,0:T(1,128)S(1)}, u32[]{:S(2)}, u32[]{:S(2)}) async-start(s32[8,128,1]{1,2,0:T(1,128)} %bitcast.8), calls=%async_computation | async-start | bytes 8192 | tf_op jit(solution)/shard_map/all_to_all | solution.py:107
  10.9 6.6 %scatter_custom_fusion.1 = f32[1024,2048]{1,0:T(8,128)} fusion(s32[256]{0:T(256)S(1)} %bitcast.96, f32[256,2048]{1,0:T(8,128)} %param.6, f32[]{:T(128)} %constant.24.clone.1), kind=kCustom, calls=%fused_computation.44 | custom fusion | bytes 8389120 | tf_op jit(solution)/shard_map/scatter | solution.py:103
  17.5 5.4 %all-to-all-start.1 = ((f32[8,128,2048]{2,1,0:T(8,128)}), f32[8,128,2048]{2,1,0:T(8,128)}, u32[]{:S(2)}, u32[]{:S(2)}) async-start(f32[8,128,2048]{2,1,0:T(8,128)} %bitcast.85), calls=%async_computation.1 | async-start | bytes 16777216 | tf_op jit(solution)/shard_map/all_to_all | solution.py:106
  22.9 7.8 %scatter_custom_fusion.3 = f32[641]{0:T(1024)S(1)} fusion(s32[1024]{0:T(1024)S(1)} %bitcast.93, f32[1024]{0:T(1024)S(1)} %broadcast.160, f32[]{:T(128)} %constant.24.clone.1), kind=kCustom, calls=%fused_computation.80 | custom fusion | flops 1024 | bytes 2568 | tf_op jit(solution)/shard_map/scatter-add | solution.py:80
  30.8 173.9 %all-to-all-done.1 = f32[8,128,2048]{2,1,0:T(8,128)} async-done(((f32[8,128,2048]{2,1,0:T(8,128)}), f32[8,128,2048]{2,1,0:T(8,128)}, u32[]{:S(2)}, u32[]{:S(2)}) %all-to-all-start.1) | async-done | bytes 8388640 | tf_op jit(solution)/shard_map/all_to_all | solution.py:106
  204.7 17.4 %scatter_custom_fusion.2 = f32[641,2048]{1,0:T(8,128)} fusion(s32[1024]{0:T(1024)S(1)} %bitcast.94, f32[1024,2048]{1,0:T(8,128)} %bitcast.11, f32[]{:T(128)} %constant.24.clone.1), kind=kCustom, calls=%fused_computation.46 | custom fusion | flops 2097152 | bytes 5251584 | tf_op jit(solution)/shard_map/scatter-add | solution.py:79
  222.1 3.3 slice_divide_fusion
  225.5 4.3 %collective-permute-start.1 = (f32[3,32,2048]{2,1,0:T(8,128)S(1)}, f32[3,32,2048]{2,1,0:T(8,128)S(1)}, u32[]{:S(2)}, u32[]{:S(2)}) collective-permute-start(f32[3,32,2048]{2,1,0:T(8,128)S(1)} %bitcast.90), channel_id=1, source_target_pairs={{1,0},{2,1},{3,2},{5,4},{6,5},{7,6},{9,8},{10,9},{11,10},{13,12},{... | collective-permute-start | bytes 2359304 | tf_op jit(solution)/shard_map/ppermute | solution.py:37
  229.8 3.2 collective-permute-start
  234.5 6.0 %collective-permute-done.1 = f32[3,32,2048]{2,1,0:T(8,128)S(1)} collective-permute-done((f32[3,32,2048]{2,1,0:T(8,128)S(1)}, f32[3,32,2048]{2,1,0:T(8,128)S(1)}, u32[]{:S(2)}, u32[]{:S(2)}) %collective-permute-start.1) | collective-permute-done | bytes 786464 | tf_op jit(solution)/shard_map/ppermute | solution.py:37
  240.6 1.2 collective-permute-done
  241.7 8.8 %fusion.7 = f32[20,32,2048]{2,1,0:T(8,128)S(1)} fusion(f32[20,32,2048]{2,1,0:T(8,128)S(1)} %bitcast.86, f32[3,32,2048]{2,1,0:T(8,128)S(1)} %collective-permute-done.1, f32[3,32,2048]{2,1,0:T(8,128)S(1)} %collective-permute-done, f32[]{:T(128)} %bitcast.20, f32[]{:T(128)} %bitcast.19, f32[]{:T(128)} %bitcast.17, f32[]{:T(128)} %bitcast.16, f32[]{:T(128)} %bitcast.15, ...), kind=kLoop, calls=%fused_computation.25 | loop fusion | flops 24903680 | bytes 12058652 | tf_op jit(solution)/shard_map/add | solution.py:74
  250.5 1.2 copy.23
  251.7 4.2 %fusion.47 = (f32[20,32,15,32]{3,2,1,0:T(8,128)S(1)}, f32[20,32,15,32]{3,2,1,0:T(8,128)}) fusion(f32[20,32,16,128]{3,2,1,0:T(8,128)S(1)} %bitcast.83), kind=kLoop, calls=%fused_computation.102 | loop fusion | bytes 4915200 | tf_op jit(solution)/shard_map/slice | solution.py:60
  256.0 13.8 %fusion = f32[20,32,16,128]{3,2,1,0:T(8,128)} fusion(f32[20,32,15,32]{3,2,1,0:T(8,128)} %get-tuple-element.6, f32[20,32,15,32]{3,2,1,0:T(8,128)S(1)} %get-tuple-element.5, f32[20,32,16,128]{3,2,1,0:T(8,128)S(1)} %bitcast.84, f32[192,128]{1,0:T(8,128)S(1)} %select_reduce_fusion), kind=kOutput, calls=%fused_computation.5 | convolution fusion | flops 3031695360 | bytes 13041664 | tf_op jit(solution)/shard_map/...ki,io->...ko/dot_general | solution.py:64
  269.8 6.7 %reshape.133 = f32[20,32,2048]{2,1,0:T(8,128)} reshape(f32[20,32,16,128]{3,2,1,0:T(8,128)} %fusion) | data formatting | bytes 10485760 | tf_op jit(solution)/shard_map/reshape | solution.py:65
  277.6 1.1 fusion.33
  281.1 1.1 fusion.30
  282.2 1.1 fusion.29
  284.5 1.1 fusion.27
  285.6 112.2 %all_to_all.26 = f32[8,20,32,256]{3,2,1,0:T(8,128)S(1)} all-to-all(f32[8,20,32,256]{3,2,1,0:T(8,128)S(1)} %fusion.27), channel_id=1, replica_groups=mesh['shot'=8,'off'=4] {'shot'}, dimensions={0} | all-to-all | bytes 10485760 | tf_op jit(solution)/shard_map/all_to_all | solution.py:13
  397.8 2.8 copy.20
  400.6 5.9 %copy.21 = f32[20,256,256]{2,1,0:T(8,128)} copy(f32[20,256,256]{1,2,0:T(8,128)} %bitcast.88) | data formatting | bytes 10485760 | tf_op jit(solution)/shard_map/transpose | solution.py:113
  (26 shorter events, 8.7 us)
Async XLA Ops:
  4.5 13.0 %all-to-all-start = ((s32[8,128,1]{1,2,0:T(1,128)}), s32[8,128,1]{1,2,0:T(1,128)S(1)}, u32[]{:S(2)}, u32[]{:S(2)}) async-start(s32[8,128,1]{1,2,0:T(1,128)} %bitcast.8), calls=%async_computation | async-start | bytes 8192 | tf_op jit(solution)/shard_map/all_to_all | solution.py:107
  17.5 187.2 %all-to-all-start.1 = ((f32[8,128,2048]{2,1,0:T(8,128)}), f32[8,128,2048]{2,1,0:T(8,128)}, u32[]{:S(2)}, u32[]{:S(2)}) async-start(f32[8,128,2048]{2,1,0:T(8,128)} %bitcast.85), calls=%async_computation.1 | async-start | bytes 16777216 | tf_op jit(solution)/shard_map/all_to_all | solution.py:106
  222.0 11.0 %copy-start = (f32[7]{0:T(128)S(1)}, f32[7]{0:T(128)}, u32[]{:S(2)}) copy-start(f32[7]{0:T(128)} %param.10) | copy-start | bytes 88
  222.1 11.7 %copy-start.1 = (f32[65]{0:T(128)S(1)}, f32[65]{0:T(128)}, u32[]{:S(2)}) copy-start(f32[65]{0:T(128)} %param.11) | copy-start | bytes 784
  225.5 15.1 %collective-permute-start.1 = (f32[3,32,2048]{2,1,0:T(8,128)S(1)}, f32[3,32,2048]{2,1,0:T(8,128)S(1)}, u32[]{:S(2)}, u32[]{:S(2)}) collective-permute-start(f32[3,32,2048]{2,1,0:T(8,128)S(1)} %bitcast.90), channel_id=1, source_target_pairs={{1,0},{2,1},{3,2},{5,4},{6,5},{7,6},{9,8},{10,9},{11,10},{13,12},{... | collective-permute-start | bytes 2359304 | tf_op jit(solution)/shard_map/ppermute | solution.py:37
  229.8 11.9 %collective-permute-start = (f32[3,32,2048]{2,1,0:T(8,128)S(1)}, f32[3,32,2048]{2,1,0:T(8,128)S(1)}, u32[]{:S(2)}, u32[]{:S(2)}) collective-permute-start(f32[3,32,2048]{2,1,0:T(8,128)S(1)} %bitcast.89), channel_id=1, source_target_pairs={{0,1},{1,2},{2,3},{4,5},{5,6},{6,7},{8,9},{9,10},{10,11},{12,13},{... | collective-permute-start | bytes 2359304 | tf_op jit(solution)/shard_map/ppermute | solution.py:35
